TPU v7x, 512 devices: a whole 4x8x8 slice. The times are simulated.
512 devices in a mesh: dp: 32 (over x_hi, z, core), expert: 16 (over y, x_lo).
Axes of the slice: x: 4 (x_hi: 2, x_lo: 2; x = x_hi * 2 + x_lo), y: 8, z: 8, core: 2. Of those that a mesh axis runs over, the one named last changes fastest.
Arguments:
- tokens: bfloat16 [65536, 1024], P(('dp', 'expert')), may hold values from -6 to 6
- grad_out: bfloat16 [65536, 1024], P(('dp', 'expert')), may hold values from -6 to 6
- routes: int32 [65536, 8], P(('dp', 'expert')), may hold values from 0 to 15, all different within a row; in each aligned block of 128 rows (0 to 127, 128 to 255, ...) at most 72 rows name the same one
- gates: float32 [65536, 8], P(('dp', 'expert')), may hold values from 0.1 to 1
- w_gate: bfloat16 [16, 1024, 384], P('expert', 'dp'), may hold values from -0.1875 to 0.1875
- w_up: bfloat16 [16, 1024, 384], P('expert', 'dp'), may hold values from -0.1875 to 0.1875
- w_down: bfloat16 [16, 384, 1024], P('expert', 'dp'), may hold values from -0.3125 to 0.3125
Outputs:
- grad_tokens: bfloat16 [65536, 1024], P(('dp', 'expert'))
- grad_gate: float32 [16, 1024, 384], P('expert', 'dp')
- grad_up: float32 [16, 1024, 384], P('expert', 'dp')
- grad_down: float32 [16, 384, 1024], P('expert', 'dp')
Inputs may be any that keep to these rules, and one draw needn't show every extreme that they name: `routes`: each row names 8 different experts. In each aligned block of 128 rows (the rows of one device) no expert is named by more than 72 rows, and in some blocks one expert is named by exactly 72 rows.
All inputs are finite; a program needn't handle non-finite values.
Results may differ from a plain program's by a relative error of at most 0.023.
Values may be sent and summed in bfloat16 or wider, within the bound.
No kernel may reach another device: no remote copies, remote signals or barrier semaphores. Data moves between devices by JAX's collectives and lax.ppermute only.
A program may use at most 64 MiB of HBM per device.

v0:
```python
import jax
import jax.numpy as jnp
from jax import lax
from jax.sharding import PartitionSpec as P

CAP = 72


def contract_last(left, right):
    return lax.dot_general(
        left, right, (((1,), (1,)), ((), ())), preferred_element_type=jnp.float32
    )


def contract_first(left, right):
    return lax.dot_general(
        left, right, (((0,), (0,)), ((), ())), preferred_element_type=jnp.float32
    )


def per_device(tokens, grad_out, routes, gates, w_gate, w_up, w_down):
    owners = lax.axis_size("expert")
    local_count = w_gate.shape[0]
    experts_all = local_count * owners
    rows_dev = tokens.shape[0]
    factor = jnp.float32((rows_dev * lax.axis_size("dp") * owners) ** (-0.5))
    matched = routes[:, :, None] == jnp.arange(experts_all, dtype=jnp.int32)[None, None, :]
    chosen = jnp.any(matched, axis=1).astype(jnp.int32)
    weight_sel = jnp.sum(jnp.where(matched, gates[:, :, None], jnp.float32(0.0)), axis=1)
    slot = jnp.cumsum(chosen, axis=0) - 1
    slot_ids = jnp.arange(CAP, dtype=jnp.int32)
    place_mask = (slot.T[:, None, :] == slot_ids[None, :, None]) & (chosen.T[:, None, :] == 1)
    place_half = place_mask.astype(jnp.bfloat16)
    place_full = place_mask.astype(jnp.float32)
    picked = jnp.einsum(
        "ecr,rd->ecd", place_half, tokens, preferred_element_type=jnp.float32
    ).astype(jnp.bfloat16)
    grad_pick = jnp.einsum("ecr,rd->ecd", place_half, grad_out, preferred_element_type=jnp.float32)
    gate_pick = jnp.einsum("ecr,re->ec", place_full, weight_sel, precision=lax.Precision.HIGHEST)
    scaled = (gate_pick[:, :, None] * grad_pick).astype(jnp.bfloat16)
    rows_all, grads_all = (
        lax.all_to_all(picked, "expert", split_axis=0, concat_axis=1, tiled=True),
        lax.all_to_all(scaled, "expert", split_axis=0, concat_axis=1, tiled=True),
    )
    full_gate, full_up, full_down = (
        lax.all_gather(w_gate, "dp", axis=1, tiled=True),
        lax.all_gather(w_up, "dp", axis=1, tiled=True),
        lax.all_gather(w_down, "dp", axis=1, tiled=True),
    )
    rows_in = rows_all[0]
    grads_in = grads_all[0]
    gate_mat = full_gate[0]
    up_mat = full_up[0]
    down_mat = full_down[0]
    gate_value = jnp.dot(rows_in, gate_mat, preferred_element_type=jnp.float32)
    up_value = jnp.dot(rows_in, up_mat, preferred_element_type=jnp.float32)
    sigmoid_gate = jax.nn.sigmoid(gate_value)
    activated = gate_value * sigmoid_gate
    hidden = (activated * up_value).astype(jnp.bfloat16)
    down_term = contract_first(hidden, grads_in)
    down_terms = [down_term]
    d_hidden = contract_last(grads_in, down_mat)
    d_up = (d_hidden * activated).astype(jnp.bfloat16)
    d_gate = (
        d_hidden * up_value * sigmoid_gate * (1.0 + gate_value * (1.0 - sigmoid_gate))
    ).astype(jnp.bfloat16)
    gate_term = contract_first(rows_in, d_gate)
    up_term = contract_first(rows_in, d_up)
    d_rows = contract_last(d_gate, gate_mat) + contract_last(d_up, up_mat)
    back_rows = [d_rows.astype(jnp.bfloat16)]
    gate_terms = [gate_term]
    up_terms = [up_term]
    gate_sum, up_sum, down_sum = (
        lax.psum_scatter(
            jnp.stack(gate_terms).astype(jnp.bfloat16), "dp", scatter_dimension=1, tiled=True
        ).astype(jnp.float32),
        lax.psum_scatter(
            jnp.stack(up_terms).astype(jnp.bfloat16), "dp", scatter_dimension=1, tiled=True
        ).astype(jnp.float32),
        lax.psum_scatter(
            jnp.stack(down_terms).astype(jnp.bfloat16), "dp", scatter_dimension=1, tiled=True
        ).astype(jnp.float32),
    )
    grad_gate = gate_sum * factor
    grad_up = up_sum * factor
    grad_down = down_sum * factor
    returned = lax.all_to_all(
        jnp.stack(back_rows), "expert", split_axis=1, concat_axis=0, tiled=True
    )
    grad_tokens = jnp.einsum(
        "ecr,ecd->rd", place_half, returned, preferred_element_type=jnp.float32
    ).astype(jnp.bfloat16)
    return (grad_tokens, grad_gate, grad_up, grad_down)


def solution(mesh):
    return jax.shard_map(
        per_device,
        mesh=mesh,
        in_specs=(
            P(("dp", "expert"), None),
            P(("dp", "expert"), None),
            P(("dp", "expert"), None),
            P(("dp", "expert"), None),
            P("expert", "dp", None),
            P("expert", "dp", None),
            P("expert", "dp", None),
        ),
        out_specs=(
            P(("dp", "expert"), None),
            P("expert", "dp", None),
            P("expert", "dp", None),
            P("expert", "dp", None),
        ),
        check_vma=False,
    )
```

profile of v0, /device:TPU:1, one launch (start us, length us, event | category | flops | bytes accessed | tf_op | source)
XLA Modules:
  0.0 539.8 jit_solution(14798313906620961361)
XLA Ops:
  7.2 0.0 copy-start
  7.2 0.7 fusion.35
  7.9 0.1 copy.30
  8.0 0.2 reduce_window_sum.11
  8.2 0.1 copy.31
  8.3 0.0 copy-done
  8.3 2.2 convolution_convert_fusion
  10.5 8.8 %all-to-all-start.1 = ((bf16[16,72,1024]{2,1,0:T(8,128)(2,1)}), bf16[16,72,1024]{2,1,0:T(8,128)(2,1)S(1)}, u32[]{:S(2)}, u32[]{:S(2)}) async-start(bf16[16,72,1024]{2,1,0:T(8,128)(2,1)} %convolution_convert_fusion), calls=%async_computation.1 | async-start | bytes 4718592 | tf_op jit(solution)/shard_map/all_to_all | solution.py:42
  19.3 0.0 copy-done.8
  19.3 0.6 fusion.22
  19.9 2.2 multiply_convert_fusion
  22.1 51.1 %all-to-all-done.1 = bf16[16,72,1024]{2,1,0:T(8,128)(2,1)S(1)} async-done(((bf16[16,72,1024]{2,1,0:T(8,128)(2,1)}), bf16[16,72,1024]{2,1,0:T(8,128)(2,1)S(1)}, u32[]{:S(2)}, u32[]{:S(2)}) %all-to-all-start.1) | async-done | bytes 2359328 | tf_op jit(solution)/shard_map/all_to_all | solution.py:42
  73.2 1.5 copy-done.1
  74.7 5.8 %all-to-all-start = ((bf16[16,72,1024]{2,1,0:T(8,128)(2,1)}), bf16[16,72,1024]{2,1,0:T(8,128)(2,1)}, u32[]{:S(2)}, u32[]{:S(2)}) async-start(bf16[16,72,1024]{2,1,0:T(8,128)(2,1)} %multiply_convert_fusion), calls=%async_computation | async-start | bytes 4718592 | tf_op jit(solution)/shard_map/all_to_all | solution.py:43
  80.6 0.0 copy-done.6
  80.6 52.4 %all_gather.11 = bf16[1,1024,384]{2,1,0:T(8,128)(2,1)S(1)} all-gather(bf16[1,32,384]{2,1,0:T(8,128)(2,1)S(1)} %copy-done.6), channel_id=1, replica_groups=mesh['dp'=32,'expert'=16] {'dp'}, dimensions={1}, use_global_device_ids=true | all-gather | bytes 811008 | tf_op jit(solution)/shard_map/all_gather | solution.py:46
  133.0 39.7 %all_gather.10 = bf16[1,1024,384]{2,1,0:T(8,128)(2,1)S(1)} all-gather(bf16[1,32,384]{2,1,0:T(8,128)(2,1)S(1)} %copy-done.7), channel_id=1, replica_groups=mesh['dp'=32,'expert'=16] {'dp'}, dimensions={1}, use_global_device_ids=true | all-gather | bytes 811008 | tf_op jit(solution)/shard_map/all_gather | solution.py:47
  172.7 44.5 %all_gather.9 = bf16[1,384,1024]{2,0,1:T(2,128)(2,1)} all-gather(bf16[1,12,1024]{2,0,1:T(2,128)(2,1)S(1)} %copy.32), channel_id=1, replica_groups=mesh['dp'=32,'expert'=16] {'dp'}, dimensions={1}, use_global_device_ids=true | all-gather | bytes 811008 | tf_op jit(solution)/shard_map/all_gather | solution.py:48
  217.3 2.6 fusion.13
  219.8 2.7 fusion.16
  222.5 0.0 all-to-all-done
  222.5 5.1 multiply_convert_fusion.2
  227.6 1.4 fusion.11
  229.0 1.4 fusion.2
  230.5 16.4 %copy.48 = bf16[1,1152,1024]{2,0,1:T(2,128)(2,1)} copy(bf16[1,1152,1024]{2,1,0:T(8,128)(2,1)S(1)} %fusion.2) | data formatting | bytes 4718592 | tf_op jit(solution)/shard_map/stack | solution.py:88
  246.9 0.5 broadcast.33
  247.4 14.2 %reduce = bf16[1152,1024]{1,0:T(8,128)(2,1)S(1)} reduce(bf16[1152,1,1024]{2,1,0:T(2,128)(2,1)} %bitcast.69, bf16[]{:T(256)} %broadcast.33), dimensions={1}, to_apply=%bitcast.68.reduce_sub_computation | reduce | bytes 4718594
  261.6 2.8 reshape.36
  264.4 8.5 %all-to-all-start.2 = ((bf16[16,2,36864]{2,1,0:T(2,128)(2,1)}), bf16[16,2,36864]{2,1,0:T(2,128)(2,1)S(1)}, u32[]{:S(2)}, u32[]{:S(2)}) async-start(bf16[16,2,36864]{2,1,0:T(2,128)(2,1)} %reshape.36), calls=%async_computation.2 | async-start | bytes 4718592 | tf_op jit(solution)/shard_map/all_to_all | solution.py:87
  272.9 0.3 reduce-scatter.8.cloned.1.call-start
  273.1 4.3 fusion.5
  277.4 0.0 reduce-scatter.8.cloned.1.call-update
  277.4 0.0 reduce-scatter.6.cloned.1.call-start
  277.5 4.1 fusion.4
  281.5 0.0 reduce-scatter.6.cloned.1.call-update
  281.6 4.0 fusion.6
  285.6 74.8 %fusion = bf16[16,1024]{1,0:T(8,128)(2,1)S(1)} fusion(bf16[1,384,1024]{2,1,0:T(8,128)(2,1)S(1)} %fusion.6), kind=kCustom, calls=%all-reduce-scatter | all-reduce-scatter fusion | flops 524289 | bytes 821248
  360.4 1.3 collective-permute-start.6
  361.7 2.9 collective-permute-start.5
  364.6 8.2 %collective-permute-start.7 = (bf16[12,1024]{1,0:T(8,128)(2,1)S(1)}, bf16[12,1024]{1,0:T(8,128)(2,1)S(1)}, u32[]{:S(2)}, u32[]{:S(2)}) collective-permute-start(bf16[12,1024]{1,0:T(8,128)(2,1)S(1)} %slice), channel_id=1, source_target_pairs={{0,128},{16,144},{32,160},{48,176},{64,192},{80,208},{96,224},{112... | collective-permute-start | bytes 73736
  372.9 1.3 collective-permute-start.4
  374.2 5.3 collective-permute-start.3
  379.5 0.0 collective-permute-done.7
  379.5 1.3 collective-permute-start.2
  380.8 0.0 collective-permute-done.6
  380.8 3.1 collective-permute-start.1
  383.9 0.0 collective-permute-done.5
  383.9 2.2 collective-permute-start
  386.1 1.3 dynamic-slice.4
  388.1 0.0 collective-permute-done.4
  388.1 0.0 collective-permute-done.3
  388.1 0.0 collective-permute-done.2
  388.1 0.0 collective-permute-done.1
  388.1 0.0 collective-permute-done
  388.1 1.2 concatenate
  389.3 0.7 copy.34
  390.0 3.5 reduce-scatter.8.cloned.1.call-done
  393.5 1.4 convert_multiply_fusion.1
  394.9 125.2 %reduce-scatter.6.cloned.1.call-done = bf16[1,32,384]{2,1,0:T(8,128)(2,1)} async-done(((bf16[1,1024,384]{2,1,0:T(8,128)(2,1)}), bf16[1,32,384]{2,1,0:T(8,128)(2,1)}) %reduce-scatter.6.cloned.1.call-update) | async-done | bytes 24592 | tf_op jit(solution)/shard_map/reduce_scatter | solution.py:74
  520.1 1.4 convert_multiply_fusion.2
  521.5 0.0 all-to-all-done.2
  521.5 6.9 %reshape.37 = bf16[1152,1,1024]{2,1,0:T(2,128)(2,1)} reshape(bf16[16,2,36864]{2,1,0:T(2,128)(2,1)S(1)} %all-to-all-done.2) | data formatting | bytes 4718592
  528.4 3.3 copy.40
  531.7 1.3 fusion.7
  (21 shorter events, 0.1 us)
Async XLA Ops:
  7.2 1.1 copy-start
  10.5 8.8 %copy-start.8 = (s32[128,8]{0,1:T(8,128)S(1)}, s32[128,8]{0,1:T(8,128)}, u32[]{:S(2)}) copy-start(s32[128,8]{0,1:T(8,128)} %param.9) | copy-start | bytes 12292
  10.5 8.8 %copy-start.9 = (f32[128,8]{0,1:T(8,128)S(1)}, f32[128,8]{0,1:T(8,128)}, u32[]{:S(2)}) copy-start(f32[128,8]{0,1:T(8,128)} %param.10) | copy-start | bytes 12292
  10.5 9.4 %copy-start.4 = (bf16[128,1024]{1,0:T(8,128)(2,1)S(1)}, bf16[128,1024]{1,0:T(8,128)(2,1)}, u32[]{:S(2)}) copy-start(bf16[128,1024]{1,0:T(8,128)(2,1)} %param.8) | copy-start | bytes 786436
  10.5 62.7 %all-to-all-start.1 = ((bf16[16,72,1024]{2,1,0:T(8,128)(2,1)}), bf16[16,72,1024]{2,1,0:T(8,128)(2,1)S(1)}, u32[]{:S(2)}, u32[]{:S(2)}) async-start(bf16[16,72,1024]{2,1,0:T(8,128)(2,1)} %convolution_convert_fusion), calls=%async_computation.1 | async-start | bytes 4718592 | tf_op jit(solution)/shard_map/all_to_all | solution.py:42
  22.1 58.5 %copy-start.5 = (bf16[1,12,1024]{2,1,0:T(8,128)(2,1)S(1)}, bf16[1,12,1024]{2,1,0:T(8,128)(2,1)}, u32[]{:S(2)}) copy-start(bf16[1,12,1024]{2,1,0:T(8,128)(2,1)} %param.13) | copy-start | bytes 73732
  22.1 58.5 %copy-start.6 = (bf16[1,32,384]{2,1,0:T(8,128)(2,1)S(1)}, bf16[1,32,384]{2,1,0:T(8,128)(2,1)}, u32[]{:S(2)}) copy-start(bf16[1,32,384]{2,1,0:T(8,128)(2,1)} %param.11) | copy-start | bytes 73732
  22.1 110.9 %copy-start.7 = (bf16[1,32,384]{2,1,0:T(8,128)(2,1)S(1)}, bf16[1,32,384]{2,1,0:T(8,128)(2,1)}, u32[]{:S(2)}) copy-start(bf16[1,32,384]{2,1,0:T(8,128)(2,1)} %param.12) | copy-start | bytes 73732
  73.2 1.5 copy-start.1
  74.7 147.8 %all-to-all-start = ((bf16[16,72,1024]{2,1,0:T(8,128)(2,1)}), bf16[16,72,1024]{2,1,0:T(8,128)(2,1)}, u32[]{:S(2)}, u32[]{:S(2)}) async-start(bf16[16,72,1024]{2,1,0:T(8,128)(2,1)} %multiply_convert_fusion), calls=%async_computation | async-start | bytes 4718592 | tf_op jit(solution)/shard_map/all_to_all | solution.py:43
  80.6 136.7 %copy-start.2 = (bf16[16,72,1024]{2,1,0:T(8,128)(2,1)S(1)}, bf16[16,72,1024]{2,1,0:T(8,128)(2,1)}, u32[]{:S(2)}) copy-start(bf16[16,72,1024]{2,1,0:T(8,128)(2,1)} %copy-done.1) | copy-start | bytes 7077892
  227.6 1.4 copy-start.3
  264.4 257.1 %all-to-all-start.2 = ((bf16[16,2,36864]{2,1,0:T(2,128)(2,1)}), bf16[16,2,36864]{2,1,0:T(2,128)(2,1)S(1)}, u32[]{:S(2)}, u32[]{:S(2)}) async-start(bf16[16,2,36864]{2,1,0:T(2,128)(2,1)} %reshape.36), calls=%async_computation.2 | async-start | bytes 4718592 | tf_op jit(solution)/shard_map/all_to_all | solution.py:87
  272.9 120.7 %reduce-scatter.8.cloned.1.call-start = ((), (), s32[]{:S(2)}) async-start(), calls=%async_computation.6 | async-start | bytes 811008 | tf_op jit(solution)/shard_map/reduce_scatter | solution.py:77
  277.4 242.7 %reduce-scatter.6.cloned.1.call-start = ((), (), s32[]{:S(2)}) async-start(), calls=%async_computation.5 | async-start | bytes 811008 | tf_op jit(solution)/shard_map/reduce_scatter | solution.py:74
  360.4 20.4 %collective-permute-start.6 = (bf16[16,1024]{1,0:T(8,128)(2,1)S(1)}, bf16[16,1024]{1,0:T(8,128)(2,1)S(1)}, u32[]{:S(2)}, u32[]{:S(2)}) collective-permute-start(bf16[16,1024]{1,0:T(8,128)(2,1)S(1)} %fusion), channel_id=1, source_target_pairs={{0,112},{16,128},{32,144},{48,160},{64,176},{80,192},{96,208},{112... | collective-permute-start | bytes 98312
  361.7 22.2 %collective-permute-start.5 = (bf16[16,1024]{1,0:T(8,128)(2,1)S(1)}, bf16[16,1024]{1,0:T(8,128)(2,1)S(1)}, u32[]{:S(2)}, u32[]{:S(2)}) collective-permute-start(bf16[16,1024]{1,0:T(8,128)(2,1)S(1)} %fusion), channel_id=1, source_target_pairs={{0,96},{16,112},{32,128},{48,144},{64,160},{80,176},{96,192},{112,... | collective-permute-start | bytes 98312
  364.6 14.9 %collective-permute-start.7 = (bf16[12,1024]{1,0:T(8,128)(2,1)S(1)}, bf16[12,1024]{1,0:T(8,128)(2,1)S(1)}, u32[]{:S(2)}, u32[]{:S(2)}) collective-permute-start(bf16[12,1024]{1,0:T(8,128)(2,1)S(1)} %slice), channel_id=1, source_target_pairs={{0,128},{16,144},{32,160},{48,176},{64,192},{80,208},{96,224},{112... | collective-permute-start | bytes 73736
  372.9 15.2 %collective-permute-start.4 = (bf16[16,1024]{1,0:T(8,128)(2,1)S(1)}, bf16[16,1024]{1,0:T(8,128)(2,1)S(1)}, u32[]{:S(2)}, u32[]{:S(2)}) collective-permute-start(bf16[16,1024]{1,0:T(8,128)(2,1)S(1)} %fusion), channel_id=1, source_target_pairs={{0,80},{16,96},{32,112},{48,128},{64,144},{80,160},{96,176},{112,1... | collective-permute-start | bytes 98312
  374.2 13.9 %collective-permute-start.3 = (bf16[16,1024]{1,0:T(8,128)(2,1)S(1)}, bf16[16,1024]{1,0:T(8,128)(2,1)S(1)}, u32[]{:S(2)}, u32[]{:S(2)}) collective-permute-start(bf16[16,1024]{1,0:T(8,128)(2,1)S(1)} %fusion), channel_id=1, source_target_pairs={{0,64},{16,80},{32,96},{48,112},{64,128},{80,144},{96,160},{112,17... | collective-permute-start | bytes 98312
  379.5 8.6 %collective-permute-start.2 = (bf16[16,1024]{1,0:T(8,128)(2,1)S(1)}, bf16[16,1024]{1,0:T(8,128)(2,1)S(1)}, u32[]{:S(2)}, u32[]{:S(2)}) collective-permute-start(bf16[16,1024]{1,0:T(8,128)(2,1)S(1)} %fusion), channel_id=1, source_target_pairs={{0,48},{16,64},{32,80},{48,96},{64,112},{80,128},{96,144},{112,160... | collective-permute-start | bytes 98312
  380.8 7.3 %collective-permute-start.1 = (bf16[16,1024]{1,0:T(8,128)(2,1)S(1)}, bf16[16,1024]{1,0:T(8,128)(2,1)S(1)}, u32[]{:S(2)}, u32[]{:S(2)}) collective-permute-start(bf16[16,1024]{1,0:T(8,128)(2,1)S(1)} %fusion), channel_id=1, source_target_pairs={{0,32},{16,48},{32,64},{48,80},{64,96},{80,112},{96,128},{112,144}... | collective-permute-start | bytes 98312
  383.9 4.2 collective-permute-start
Sparse Core Ops, SparseCore 0:
  278.3 115.2 reduce-scatter.7
  398.1 121.9 reduce-scatter.5
where the time goes:
time: 545 us; the launch traced here: 540 us
  blocking collectives  211 us (39%)
  waiting for transfers between devices  180 us (33%)
  starting transfers between devices  49.1 us (9%)
  local copies, waits for them, and re-layouts  34.8 us (6%)
  matrix products  31.7 us (6%)
  other arithmetic  17.9 us (3%)
  between operations  15 us (3%)
    reduce_scatter x1, waiting for transfers between devices, per_device(): lax.psum_scatter(jnp.stack(gate_terms).astype(jnp.bfloat16), 'dp', scatte...  125 us
    unnamed x1, blocking collectives  74.8 us
    all_gather x1, blocking collectives, per_device(): lax.all_gather(w_gate, 'dp', axis=1, tiled=True)  52.4 us
    all_to_all x1, waiting for transfers between devices, per_device(): lax.all_to_all(picked, 'expert', split_axis=0, concat_axis=1, tiled=True)  51.1 us
    all_gather x1, blocking collectives, per_device(): lax.all_gather(w_down, 'dp', axis=1, tiled=True)  44.5 us
    all_gather x1, blocking collectives, per_device(): lax.all_gather(w_up, 'dp', axis=1, tiled=True)  39.7 us
    unnamed x8, starting transfers between devices  25.6 us
    unnamed x29, local copies, waits for them, and re-layouts  18.2 us
  transfers between devices with their start and end apart: 13, of which 3 were waited for; matrix products, arithmetic and copies ran while one was open for 19% of the time, Pallas kernels for 0%

commit v1 on v0

v1 whole, which is shorter than its diff:
```python
import jax
import jax.numpy as jnp
import numpy as np
from jax import lax
from jax.sharding import Mesh
from jax.sharding import PartitionSpec as P

CAP = 72
DP = ("x_hi", "z", "core")
EX = ("y", "x_lo")


def contract_last(left, right):
    return lax.dot_general(
        left, right, (((1,), (1,)), ((), ())), preferred_element_type=jnp.float32
    )


def contract_first(left, right):
    return lax.dot_general(
        left, right, (((0,), (0,)), ((), ())), preferred_element_type=jnp.float32
    )


def make_body(n_dp, owners):
    def per_device(tokens, grad_out, routes, gates, w_gate, w_up, w_down):
        local_count = w_gate.shape[0]
        experts_all = local_count * owners
        rows_dev, dmodel = tokens.shape
        dshard, hdim = w_gate.shape[1], w_gate.shape[2]
        hshard = w_down.shape[1]
        factor = jnp.float32((rows_dev * n_dp * owners) ** (-0.5))

        down_flat = w_down[0].reshape(dshard, hdim)
        packed = jnp.stack([w_gate[0], w_up[0], down_flat])
        gathered = lax.all_gather(packed, DP, axis=0, tiled=False)
        gate_mat = gathered[:, 0].reshape(n_dp * dshard, hdim)
        up_mat = gathered[:, 1].reshape(n_dp * dshard, hdim)
        down_mat = gathered[:, 2].reshape(n_dp * hshard, dmodel)

        matched = routes[:, :, None] == jnp.arange(experts_all, dtype=jnp.int32)[None, None, :]
        chosen = jnp.any(matched, axis=1).astype(jnp.int32)
        weight_sel = jnp.sum(jnp.where(matched, gates[:, :, None], jnp.float32(0.0)), axis=1)
        slot = jnp.cumsum(chosen, axis=0) - 1
        slot_ids = jnp.arange(CAP, dtype=jnp.int32)
        place_mask = (slot.T[:, None, :] == slot_ids[None, :, None]) & (chosen.T[:, None, :] == 1)
        place_half = place_mask.astype(jnp.bfloat16)
        place_full = place_mask.astype(jnp.float32)
        picked = jnp.einsum(
            "ecr,rd->ecd", place_half, tokens, preferred_element_type=jnp.float32
        ).astype(jnp.bfloat16)
        rows_in = lax.all_to_all(picked, EX, split_axis=0, concat_axis=0, tiled=True)
        grad_pick = jnp.einsum("ecr,rd->ecd", place_half, grad_out, preferred_element_type=jnp.float32)
        gate_pick = jnp.einsum("ecr,re->ec", place_full, weight_sel, precision=lax.Precision.HIGHEST)
        scaled = (gate_pick[:, :, None] * grad_pick).astype(jnp.bfloat16)
        grads_in = lax.all_to_all(scaled, EX, split_axis=0, concat_axis=0, tiled=True)
        rows_in = rows_in.reshape(owners * CAP, dmodel)
        grads_in = grads_in.reshape(owners * CAP, dmodel)

        gate_value = jnp.dot(rows_in, gate_mat, preferred_element_type=jnp.float32)
        up_value = jnp.dot(rows_in, up_mat, preferred_element_type=jnp.float32)
        sigmoid_gate = jax.nn.sigmoid(gate_value)
        activated = gate_value * sigmoid_gate
        hidden = (activated * up_value).astype(jnp.bfloat16)
        d_hidden = contract_last(grads_in, down_mat)
        d_up = (d_hidden * activated).astype(jnp.bfloat16)
        d_gate = (
            d_hidden * up_value * sigmoid_gate * (1.0 + gate_value * (1.0 - sigmoid_gate))
        ).astype(jnp.bfloat16)
        d_rows = contract_last(d_gate, gate_mat) + contract_last(d_up, up_mat)
        back = d_rows.astype(jnp.bfloat16).reshape(owners, CAP, dmodel)
        returned = lax.all_to_all(back, EX, split_axis=0, concat_axis=0, tiled=True)

        gate_term = contract_first(rows_in, d_gate).astype(jnp.bfloat16)
        up_term = contract_first(rows_in, d_up).astype(jnp.bfloat16)
        down_term = contract_first(hidden, grads_in).astype(jnp.bfloat16)
        parts = jnp.stack(
            [
                gate_term.reshape(n_dp, dshard, hdim),
                up_term.reshape(n_dp, dshard, hdim),
                down_term.reshape(n_dp, dshard, hdim),
            ],
            axis=1,
        )
        summed = lax.psum_scatter(parts, DP, scatter_dimension=0, tiled=True)
        grad_gate = summed[:, 0].astype(jnp.float32) * factor
        grad_up = summed[:, 1].astype(jnp.float32) * factor
        grad_down = summed[:, 2].reshape(1, hshard, dmodel).astype(jnp.float32) * factor

        grad_tokens = jnp.einsum(
            "ecr,ecd->rd", place_half, returned, preferred_element_type=jnp.float32
        ).astype(jnp.bfloat16)
        return (grad_tokens, grad_gate, grad_up, grad_down)

    return per_device


def solution(mesh):
    n_dp, owners = mesh.devices.shape
    fine = Mesh(
        np.asarray(mesh.devices).reshape(2, n_dp // 4, 2, owners // 2, 2),
        ("x_hi", "z", "core", "y", "x_lo"),
    )
    rows = P(DP + EX, None)
    weights = P(EX, DP, None)
    return jax.shard_map(
        make_body(n_dp, owners),
        mesh=fine,
        in_specs=(rows, rows, rows, rows, weights, weights, weights),
        out_specs=(rows, weights, weights, weights),
        check_vma=False,
    )
```

time: 545 us -> 309 us (0.57)
  blocking collectives: 211 us -> 0 us
  waiting for transfers between devices: 180 us -> 222 us
  starting transfers between devices: 49.1 us -> 21.5 us
  local copies, waits for them, and re-layouts: 34.8 us -> 8.05 us
  other arithmetic: 17.9 us -> 4.74 us
    all_gather x3 -> x0, blocking collectives: 137 us -> none  [the longest x1 52.4 us: per_device(): lax.all_gather(w_gate, 'dp', axis=1, tiled=True)]
    unnamed x1 -> x0, blocking collectives: 74.8 us -> none
    all_gather x0 -> x1, waiting for transfers between devices: none -> 43.5 us  [per_device(): gathered = lax.all_gather(packed, DP, axis=0, tiled=False)]
    unnamed x8 -> x0, starting transfers between devices: 25.6 us -> none
    unnamed x29 -> x28, local copies, waits for them, and re-layouts: 18.2 us -> 1.49 us
    unnamed x1 -> x0, other arithmetic: 14.2 us -> none
    another operation x1 -> x3, local copies, waits for them, and re-layouts: 16.4 us -> 3.87 us  [the longest x1 2.02 us: per_device(): jnp.stack([gate_term.reshape(n_dp, dshard, hdim), up_term.reshape(n_dp, d...]
    reduce_scatter x2 -> x1, waiting for transfers between devices: 129 us -> 128 us  [per_device(): summed = lax.psum_scatter(parts, DP, scatter_dimension=0, tiled=True)]
  transfers between devices with their start and end apart: 13 -> 5, of which waited for: 3 -> 3; matrix products, arithmetic and copies ran while one was open for 19% -> 9% of each run, Pallas kernels for 0% -> 0%
where the time goes in v1:
time: 309 us; the launch traced here: 304 us
  waiting for transfers between devices  222 us (72%)
  matrix products  33.9 us (11%)
  starting transfers between devices  21.5 us (7%)
  between operations  14.2 us (5%)
  local copies, waits for them, and re-layouts  8.05 us (3%)
  other arithmetic  4.74 us (2%)
    reduce_scatter x1, waiting for transfers between devices, per_device(): summed = lax.psum_scatter(parts, DP, scatter_dimension=0, tiled=True)  128 us
    all_to_all x1, waiting for transfers between devices, per_device(): lax.all_to_all(picked, EX, split_axis=0, concat_axis=0, tiled=True)  50.3 us
    all_gather x1, waiting for transfers between devices, per_device(): gathered = lax.all_gather(packed, DP, axis=0, tiled=False)  43.5 us
    dot_general x3, matrix products, contract_first(): lax.dot_general(left, right, (((0,), (0,)), ((), ())), preferred_element_...  12.5 us
    all_to_all x1, starting transfers between devices, per_device(): lax.all_to_all(picked, EX, split_axis=0, concat_axis=0, tiled=True)  8.81 us
    dot_general x3, matrix products, contract_last(): lax.dot_general(left, right, (((1,), (1,)), ((), ())), preferred_element_...  7.95 us
    all_to_all x1, starting transfers between devices, per_device(): returned = lax.all_to_all(back, EX, split_axis=0, concat_axis=0, tiled=True)  6.57 us
  transfers between devices with their start and end apart: 5, of which 3 were waited for; matrix products, arithmetic and copies ran while one was open for 9% of the time, Pallas kernels for 0%

profile of v1, /device:TPU:1, one launch (start us, length us, event | category | flops | bytes accessed | tf_op | source)
XLA Modules:
  0.0 304.4 jit_solution(4299434293220132040)
XLA Ops:
  7.2 0.0 copy-start
  7.2 0.7 fusion.20
  7.9 0.1 copy.25
  8.0 0.2 reduce_window_sum.11
  8.2 0.1 copy.26
  8.3 0.0 copy-done
  8.3 2.2 convolution_convert_fusion
  10.5 0.0 copy-start.7
  10.5 0.0 copy-start.8
  10.5 0.0 copy-start.9
  10.5 0.0 copy-start.10
  10.5 0.0 copy-start.11
  10.5 0.0 copy-start.6
  10.5 8.8 %all-to-all-start.1 = ((bf16[16,72,1024]{2,1,0:T(8,128)(2,1)}), bf16[16,72,1024]{2,1,0:T(8,128)(2,1)S(1)}, u32[]{:S(2)}, u32[]{:S(2)}) async-start(bf16[16,72,1024]{2,1,0:T(8,128)(2,1)} %convolution_convert_fusion), calls=%async_computation.1 | async-start | bytes 4718592 | tf_op jit(solution)/shard_map/all_to_all | solution.py:52
  19.3 0.0 all-gather.3.cloned.1.call-start
  19.4 0.0 copy-done.7
  19.5 0.0 copy-done.8
  19.5 0.0 copy-done.9
  19.5 0.6 pad_maximum_fusion.1
  20.1 0.0 all-gather.3.cloned.1.call-update
  20.2 0.0 copy-done.10
  20.2 0.0 copy-done.11
  20.2 0.6 fusion.7
  20.8 0.0 copy-done.6
  20.8 2.2 multiply_convert_fusion
  23.0 50.3 %all-to-all-done.1 = bf16[16,72,1024]{2,1,0:T(8,128)(2,1)S(1)} async-done(((bf16[16,72,1024]{2,1,0:T(8,128)(2,1)}), bf16[16,72,1024]{2,1,0:T(8,128)(2,1)S(1)}, u32[]{:S(2)}, u32[]{:S(2)}) %all-to-all-start.1) | async-done | bytes 2359328 | tf_op jit(solution)/shard_map/all_to_all | solution.py:52
  73.3 0.0 copy-start.1
  73.3 1.4 copy-done.1
  74.7 5.8 %all-to-all-start = ((bf16[16,72,1024]{2,1,0:T(8,128)(2,1)}), bf16[16,72,1024]{2,1,0:T(8,128)(2,1)}, u32[]{:S(2)}, u32[]{:S(2)}) async-start(bf16[16,72,1024]{2,1,0:T(8,128)(2,1)} %multiply_convert_fusion), calls=%async_computation | async-start | bytes 4718592 | tf_op jit(solution)/shard_map/all_to_all | solution.py:56
  80.6 43.5 %all-gather.3.cloned.1.call-done = bf16[96,32,384]{2,1,0:T(8,128)(2,1)} async-done(((bf16[3,32,384]{2,1,0:T(8,128)(2,1)}), bf16[96,32,384]{2,1,0:T(8,128)(2,1)}) %all-gather.3.cloned.1.call-update) | async-done | bytes 2359312 | tf_op jit(solution)/shard_map/all_gather | solution.py:36
  124.1 1.9 fusion.22
  125.9 1.8 reshape_squeeze.10
  127.7 0.0 copy-start.2
  127.7 4.4 %fusion.23 = f32[1152,384]{1,0:T(8,128)} fusion(bf16[1152,1024]{1,0:T(8,128)(2,1)} %bitcast.63, bf16[1024,384]{1,0:T(8,128)(2,1)S(1)} %bitcast.58), kind=kOutput, calls=%fused_computation.39 | convolution fusion | flops 905969664 | bytes 4915200 | tf_op jit(solution)/shard_map/dot_general | solution.py:61
  132.2 0.0 copy-done.2
  132.2 2.7 fusion.24
  134.9 0.0 all-to-all-done
  134.9 0.0 copy-start.5
  134.9 0.0 copy-start.12
  134.9 0.0 copy-start.13
  134.9 5.0 %convolution_convert_fusion.1 = bf16[384,1024]{1,0:T(8,128)(2,1)} fusion(bf16[1152,1024]{1,0:T(8,128)(2,1)} %bitcast.7, f32[1152,384]{1,0:T(8,128)} %fusion.23, f32[1152,384]{1,0:T(8,128)} %fusion.24), kind=kOutput, calls=%fused_computation.10 | convolution fusion | flops 909017088 | bytes 6684672 | tf_op jit(solution)/shard_map/dot_general | solution.py:20
  139.9 0.0 copy-done.5
  139.9 0.0 copy-done.12
  139.9 0.0 copy-done.13
  139.9 3.7 %multiply_convert_fusion.2 = (bf16[1152,384]{1,0:T(8,128)(2,1)S(1)}, bf16[1152,384]{1,0:T(8,128)(2,1)S(1)}) fusion(f32[1152,384]{1,0:T(8,128)S(1)} %copy-done.13, f32[1152,384]{1,0:T(8,128)S(1)} %copy-done.12, bf16[1152,1024]{1,0:T(8,128)(2,1)} %bitcast.7, bf16[384,1024]{1,0:T(8,128)(2,1)S(1)} %copy-done.5), kind=kOutput, calls=%fused_computation.6 | convolution fusion | flops 911720448 | bytes 8454144 | tf_op jit(solution)/shard_map/dot_general | solution.py:14
  143.6 0.0 copy-start.3
  143.6 1.4 fusion.25
  145.0 0.0 copy-done.3
  145.0 2.8 fusion
  147.9 6.6 %all-to-all-start.2 = ((bf16[16,72,1024]{2,1,0:T(8,128)(2,1)}), bf16[16,72,1024]{2,1,0:T(8,128)(2,1)S(1)}, u32[]{:S(2)}, u32[]{:S(2)}) async-start(bf16[16,72,1024]{2,1,0:T(8,128)(2,1)} %bitcast.57), calls=%async_computation.2 | async-start | bytes 4718592 | tf_op jit(solution)/shard_map/all_to_all | solution.py:72
  154.5 0.2 reduce-scatter.2.cloned.1.call-start
  154.7 4.1 %convolution_convert_fusion.3 = bf16[1024,384]{1,0:T(8,128)(2,1)} fusion(bf16[1152,1024]{1,0:T(8,128)(2,1)} %bitcast.64, bf16[1152,384]{1,0:T(8,128)(2,1)S(1)} %get-tuple-element.5), kind=kOutput, calls=%fused_computation.12 | convolution fusion | flops 906362880 | bytes 4030464 | tf_op jit(solution)/shard_map/dot_general | solution.py:20
  158.8 2.0 stack_reshape.11
  160.8 0.0 copy-start.4
  160.8 3.4 %convolution_convert_fusion.2 = bf16[1024,384]{1,0:T(8,128)(2,1)S(1)} fusion(bf16[1152,1024]{1,0:T(8,128)(2,1)} %bitcast.65, bf16[1152,384]{1,0:T(8,128)(2,1)} %copy-done.3), kind=kOutput, calls=%fused_computation.11 | convolution fusion | flops 906362880 | bytes 4030464 | tf_op jit(solution)/shard_map/dot_general | solution.py:20
  164.3 0.0 copy-done.4
  164.3 1.7 pad_maximum_fusion
  166.0 0.0 reduce-scatter.2.cloned.1.call-update
  166.0 128.1 %reduce-scatter.2.cloned.1.call-done = bf16[1,3,32,384]{3,2,1,0:T(8,128)(2,1)} async-done(((bf16[32,3,32,384]{3,2,1,0:T(8,128)(2,1)}), bf16[1,3,32,384]{3,2,1,0:T(8,128)(2,1)}) %reduce-scatter.2.cloned.1.call-update) | async-done | bytes 73744 | tf_op jit(solution)/shard_map/reduce_scatter | solution.py:85
  294.2 1.4 convert_multiply_fusion
  295.6 0.7 mul.86
  296.2 0.0 all-to-all-done.2
  296.2 1.3 fusion.2
  (4 shorter events, 0.1 us)
Async XLA Ops:
  7.2 1.1 copy-start
  10.5 8.9 %copy-start.7 = (bf16[1,12,1024]{2,1,0:T(8,128)(2,1)S(1)}, bf16[1,12,1024]{2,1,0:T(8,128)(2,1)}, u32[]{:S(2)}) copy-start(bf16[1,12,1024]{2,1,0:T(8,128)(2,1)} %param.13) | copy-start | bytes 73732
  10.5 9.0 %copy-start.8 = (bf16[1,32,384]{2,1,0:T(8,128)(2,1)S(1)}, bf16[1,32,384]{2,1,0:T(8,128)(2,1)}, u32[]{:S(2)}) copy-start(bf16[1,32,384]{2,1,0:T(8,128)(2,1)} %param.12) | copy-start | bytes 73732
  10.5 9.0 %copy-start.9 = (bf16[1,32,384]{2,1,0:T(8,128)(2,1)S(1)}, bf16[1,32,384]{2,1,0:T(8,128)(2,1)}, u32[]{:S(2)}) copy-start(bf16[1,32,384]{2,1,0:T(8,128)(2,1)} %param.11) | copy-start | bytes 73732
  10.5 9.7 %copy-start.10 = (s32[128,8]{0,1:T(8,128)S(1)}, s32[128,8]{0,1:T(8,128)}, u32[]{:S(2)}) copy-start(s32[128,8]{0,1:T(8,128)} %param.9) | copy-start | bytes 12292
  10.5 9.7 %copy-start.11 = (f32[128,8]{0,1:T(8,128)S(1)}, f32[128,8]{0,1:T(8,128)}, u32[]{:S(2)}) copy-start(f32[128,8]{0,1:T(8,128)} %param.10) | copy-start | bytes 12292
  10.5 10.2 %copy-start.6 = (bf16[128,1024]{1,0:T(8,128)(2,1)S(1)}, bf16[128,1024]{1,0:T(8,128)(2,1)}, u32[]{:S(2)}) copy-start(bf16[128,1024]{1,0:T(8,128)(2,1)} %param.8) | copy-start | bytes 786436
  10.5 62.8 %all-to-all-start.1 = ((bf16[16,72,1024]{2,1,0:T(8,128)(2,1)}), bf16[16,72,1024]{2,1,0:T(8,128)(2,1)S(1)}, u32[]{:S(2)}, u32[]{:S(2)}) async-start(bf16[16,72,1024]{2,1,0:T(8,128)(2,1)} %convolution_convert_fusion), calls=%async_computation.1 | async-start | bytes 4718592 | tf_op jit(solution)/shard_map/all_to_all | solution.py:52
  19.3 104.7 %all-gather.3.cloned.1.call-start = ((), (), s32[]{:S(2)}) async-start(), calls=%async_computation.5 | async-start | bytes 2433024 | tf_op jit(solution)/shard_map/all_gather | solution.py:36
  73.3 1.4 copy-start.1
  74.7 60.1 %all-to-all-start = ((bf16[16,72,1024]{2,1,0:T(8,128)(2,1)}), bf16[16,72,1024]{2,1,0:T(8,128)(2,1)}, u32[]{:S(2)}, u32[]{:S(2)}) async-start(bf16[16,72,1024]{2,1,0:T(8,128)(2,1)} %multiply_convert_fusion), calls=%async_computation | async-start | bytes 4718592 | tf_op jit(solution)/shard_map/all_to_all | solution.py:56
  127.7 4.4 %copy-start.2 = (bf16[16,72,1024]{2,1,0:T(8,128)(2,1)S(1)}, bf16[16,72,1024]{2,1,0:T(8,128)(2,1)}, u32[]{:S(2)}) copy-start(bf16[16,72,1024]{2,1,0:T(8,128)(2,1)} %copy-done.1) | copy-start | bytes 7077892
  134.9 5.0 %copy-start.5 = (bf16[384,1024]{1,0:T(8,128)(2,1)S(1)}, bf16[384,1024]{1,0:T(8,128)(2,1)}, u32[]{:S(2)}) copy-start(bf16[384,1024]{1,0:T(8,128)(2,1)} %reshape_squeeze.10) | copy-start | bytes 2359300
  134.9 5.0 %copy-start.12 = (f32[1152,384]{1,0:T(8,128)S(1)}, f32[1152,384]{1,0:T(8,128)}, u32[]{:S(2)}) copy-start(f32[1152,384]{1,0:T(8,128)} %fusion.23) | copy-start | bytes 5308420
  134.9 5.0 %copy-start.13 = (f32[1152,384]{1,0:T(8,128)S(1)}, f32[1152,384]{1,0:T(8,128)}, u32[]{:S(2)}) copy-start(f32[1152,384]{1,0:T(8,128)} %fusion.24) | copy-start | bytes 5308420
  143.6 1.4 copy-start.3
  147.9 148.4 %all-to-all-start.2 = ((bf16[16,72,1024]{2,1,0:T(8,128)(2,1)}), bf16[16,72,1024]{2,1,0:T(8,128)(2,1)S(1)}, u32[]{:S(2)}, u32[]{:S(2)}) async-start(bf16[16,72,1024]{2,1,0:T(8,128)(2,1)} %bitcast.57), calls=%async_computation.2 | async-start | bytes 4718592 | tf_op jit(solution)/shard_map/all_to_all | solution.py:72
  154.5 139.7 %reduce-scatter.2.cloned.1.call-start = ((), (), s32[]{:S(2)}) async-start(), calls=%async_computation.4 | async-start | bytes 2433024 | tf_op jit(solution)/shard_map/reduce_scatter | solution.py:85
  160.8 3.5 %copy-start.4 = (bf16[1024,384]{1,0:T(8,128)(2,1)S(1)}, bf16[1024,384]{1,0:T(8,128)(2,1)}, u32[]{:S(2)}) copy-start(bf16[1024,384]{1,0:T(8,128)(2,1)} %convolution_convert_fusion.3) | copy-start | bytes 2359300
Sparse Core Ops, SparseCore 0:
  24.1 99.9 all-gather.2
  166.1 127.9 reduce-scatter.1

commit v2 on v1

--- a/solution.py
+++ b/solution.py
@@ -32,8 +32,12 @@
         factor = jnp.float32((rows_dev * n_dp * owners) ** (-0.5))
 
         down_flat = w_down[0].reshape(dshard, hdim)
-        packed = jnp.stack([w_gate[0], w_up[0], down_flat])
-        gathered = lax.all_gather(packed, DP, axis=0, tiled=False)
+        packed = jnp.stack([w_gate[0], w_up[0], down_flat])[None, None, None]
+        gathered = lax.all_gather(packed, "x_hi", axis=2, tiled=True)
+        gathered = lax.all_gather(gathered, "z", axis=1, tiled=True)
+        gathered = lax.all_gather(gathered, "core", axis=0, tiled=True)
+        gathered = jnp.transpose(gathered, (2, 1, 0, 3, 4, 5))
+        gathered = gathered.reshape((n_dp,) + packed.shape[3:])
         gate_mat = gathered[:, 0].reshape(n_dp * dshard, hdim)
         up_mat = gathered[:, 1].reshape(n_dp * dshard, hdim)
         down_mat = gathered[:, 2].reshape(n_dp * hshard, dmodel)
@@ -82,7 +86,12 @@
             ],
             axis=1,
         )
-        summed = lax.psum_scatter(parts, DP, scatter_dimension=0, tiled=True)
+        parts = parts.reshape((2, n_dp // 4, 2) + parts.shape[1:])
+        parts = jnp.transpose(parts, (2, 1, 0, 3, 4, 5))
+        parts = lax.psum_scatter(parts, "core", scatter_dimension=0, tiled=True)
+        parts = lax.psum_scatter(parts, "z", scatter_dimension=1, tiled=True)
+        parts = lax.psum_scatter(parts, "x_hi", scatter_dimension=2, tiled=True)
+        summed = parts.reshape(parts.shape[2:])
         grad_gate = summed[:, 0].astype(jnp.float32) * factor
         grad_up = summed[:, 1].astype(jnp.float32) * factor
         grad_down = summed[:, 2].reshape(1, hshard, dmodel).astype(jnp.float32) * factor

time: 309 us -> 250 us (0.81); the launches traced: 304 us -> 250 us
  waiting for transfers between devices: 222 us -> 165 us
  blocking collectives: 0 us -> 7.29 us
    reduce_scatter x1 -> x3, waiting for transfers between devices: 128 us -> 76.9 us  [the longest x1 41.9 us: per_device(): parts = lax.psum_scatter(parts, 'z', scatter_dimension=1, tiled=True)]
    all_gather x1 -> x2, waiting for transfers between devices: 43.5 us -> 27.6 us  [the longest x1 27.6 us: per_device(): gathered = lax.all_gather(gathered, 'core', axis=0, tiled=True)]
    all_to_all x1, waiting for transfers between devices: 0.01 us -> 15.6 us  [per_device(): lax.all_to_all(scaled, EX, split_axis=0, concat_axis=0, tiled=True)]
    all_gather x0 -> x1, blocking collectives: none -> 7.29 us  [per_device(): gathered = lax.all_gather(packed, 'x_hi', axis=2, tiled=True)]
    all_to_all x1, waiting for transfers between devices: 50.3 us -> 43.6 us  [per_device(): lax.all_to_all(picked, EX, split_axis=0, concat_axis=0, tiled=True)]
    transpose x0 -> x1, other arithmetic: none -> 3.14 us  [per_device(): parts = jnp.transpose(parts, (2, 1, 0, 3, 4, 5))]
  transfers between devices with their start and end apart: 5 -> 8, of which waited for: 3 -> 7; matrix products, arithmetic and copies ran while one was open for 9% -> 7% of each run, Pallas kernels for 0% -> 0%
where the time goes in v2:
time: 250 us
  waiting for transfers between devices  165 us (66%)
  matrix products  31.4 us (13%)
  starting transfers between devices  20.8 us (8%)
  between operations  14 us (6%)
  blocking collectives  7.29 us (3%)
  local copies, waits for them, and re-layouts  5.73 us (2%)
  other arithmetic  5.52 us (2%)
    all_to_all x1, waiting for transfers between devices, per_device(): lax.all_to_all(picked, EX, split_axis=0, concat_axis=0, tiled=True)  43.6 us
    reduce_scatter x1, waiting for transfers between devices, per_device(): parts = lax.psum_scatter(parts, 'z', scatter_dimension=1, tiled=True)  41.9 us
    all_gather x1, waiting for transfers between devices, per_device(): gathered = lax.all_gather(gathered, 'core', axis=0, tiled=True)  27.6 us
    reduce_scatter x1, waiting for transfers between devices, per_device(): parts = lax.psum_scatter(parts, 'x_hi', scatter_dimension=2, tiled=True)  22.8 us
    all_to_all x1, waiting for transfers between devices, per_device(): lax.all_to_all(scaled, EX, split_axis=0, concat_axis=0, tiled=True)  15.6 us
    reduce_scatter x1, waiting for transfers between devices, per_device(): parts = lax.psum_scatter(parts, 'core', scatter_dimension=0, tiled=True)  12.2 us
    dot_general x3, matrix products, contract_first(): lax.dot_general(left, right, (((0,), (0,)), ((), ())), preferred_element_...  9.84 us
    all_to_all x1, starting transfers between devices, per_device(): lax.all_to_all(picked, EX, split_axis=0, concat_axis=0, tiled=True)  8.81 us
  transfers between devices with their start and end apart: 8, of which 7 were waited for; matrix products, arithmetic and copies ran while one was open for 7% of the time, Pallas kernels for 0%

profile of v2, /device:TPU:1, one launch (start us, length us, event | category | flops | bytes accessed | tf_op | source)
XLA Modules:
  0.0 249.5 jit_solution(3264913583734512116)
XLA Ops:
  7.2 0.0 copy-start
  7.2 0.7 fusion.20
  7.9 0.1 copy.32
  8.0 0.2 reduce_window_sum.11
  8.2 0.1 copy.33
  8.3 0.0 copy-done
  8.3 2.2 convolution_convert_fusion
  10.5 0.0 copy-start.11
  10.5 0.0 copy-start.6
  10.5 8.8 %all-to-all-start.1 = ((bf16[16,72,1024]{2,1,0:T(8,128)(2,1)}), bf16[16,72,1024]{2,1,0:T(8,128)(2,1)S(1)}, u32[]{:S(2)}, u32[]{:S(2)}) async-start(bf16[16,72,1024]{2,1,0:T(8,128)(2,1)} %convolution_convert_fusion), calls=%async_computation.1 | async-start | bytes 4718592 | tf_op jit(solution)/shard_map/all_to_all | solution.py:56
  19.4 0.0 all-gather.4.cloned.1.call-start
  19.4 0.0 copy-done.7
  19.5 0.0 copy-done.8
  19.5 0.0 copy-done.9
  19.5 7.3 %all-gather = bf16[6,32,384]{2,1,0:T(8,128)(2,1)} all-gather(bf16[3,32,384]{2,1,0:T(8,128)(2,1)S(1)} %pad_maximum_fusion.1), channel_id=2, replica_groups=mesh['x_hi'=2,'z'=8,'core'=2,'y'=8,'x_lo'=2] {'x_hi'}, dimensions={0}, use_global_device_ids=true | all-gather | bytes 221184 | tf_op jit(solution)/shard_map/all_gather | solution.py:36
  26.8 0.0 all-gather.4.cloned.1.call-update
  26.8 0.0 copy-done.10
  26.8 0.0 copy-done.11
  26.9 0.6 fusion.7
  27.4 0.0 copy-done.6
  27.4 2.2 multiply_convert_fusion
  29.7 43.6 %all-to-all-done.1 = bf16[16,72,1024]{2,1,0:T(8,128)(2,1)S(1)} async-done(((bf16[16,72,1024]{2,1,0:T(8,128)(2,1)}), bf16[16,72,1024]{2,1,0:T(8,128)(2,1)S(1)}, u32[]{:S(2)}, u32[]{:S(2)}) %all-to-all-start.1) | async-done | bytes 2359328 | tf_op jit(solution)/shard_map/all_to_all | solution.py:56
  73.3 5.8 %all-to-all-start = ((bf16[16,72,1024]{2,1,0:T(8,128)(2,1)}), bf16[16,72,1024]{2,1,0:T(8,128)(2,1)}, u32[]{:S(2)}, u32[]{:S(2)}) async-start(bf16[16,72,1024]{2,1,0:T(8,128)(2,1)} %multiply_convert_fusion), calls=%async_computation | async-start | bytes 4718592 | tf_op jit(solution)/shard_map/all_to_all | solution.py:60
  79.1 0.0 all-gather.6.cloned.1.call-start
  79.2 0.0 all-gather.4.cloned.1.call-done
  79.2 0.0 copy-done.1
  79.2 0.7 all-gather.6.cloned.1.call-update
  79.9 0.2 reduce-scatter.4.cloned.1.call-start
  80.1 27.6 %all-gather.6.cloned.1.call-done = bf16[2,8,2,3,32,384]{5,4,3,0,1,2:T(8,128)(2,1)} async-done(((bf16[1,8,2,3,32,384]{5,4,3,0,1,2:T(8,128)(2,1)}), bf16[2,8,2,3,32,384]{5,4,3,0,1,2:T(8,128)(2,1)}) %all-gather.6.cloned.1.call-update) | async-done | bytes 2359312 | tf_op jit(solution)/shard_map/all_gather | solution.py:38
  107.7 1.9 fusion.22
  109.6 0.9 reshape_squeeze.10
  110.5 0.0 copy-start.2
  110.5 4.4 %fusion.23 = f32[1152,384]{1,0:T(8,128)} fusion(bf16[1152,1024]{1,0:T(8,128)(2,1)} %bitcast.63, bf16[1024,384]{1,0:T(8,128)(2,1)S(1)} %bitcast.59), kind=kOutput, calls=%fused_computation.40 | convolution fusion | flops 905969664 | bytes 4915200 | tf_op jit(solution)/shard_map/dot_general | solution.py:65
  114.9 0.0 copy-done.2
  114.9 2.7 %fusion.24 = f32[1152,384]{1,0:T(8,128)} fusion(bf16[1152,1024]{1,0:T(8,128)(2,1)S(1)} %bitcast.64, bf16[1024,384]{1,0:T(8,128)(2,1)S(1)} %bitcast.61), kind=kOutput, calls=%fused_computation.41 | convolution fusion | flops 905969664 | bytes 4915200 | tf_op jit(solution)/shard_map/dot_general | solution.py:64
  117.6 15.6 %all-to-all-done = bf16[16,72,1024]{2,1,0:T(8,128)(2,1)} async-done(((bf16[16,72,1024]{2,1,0:T(8,128)(2,1)}), bf16[16,72,1024]{2,1,0:T(8,128)(2,1)}, u32[]{:S(2)}, u32[]{:S(2)}) %all-to-all-start) | async-done | bytes 2359328 | tf_op jit(solution)/shard_map/all_to_all | solution.py:60
  133.2 5.0 %convolution_convert_fusion.1 = bf16[384,1024]{1,0:T(8,128)(2,1)} fusion(bf16[1152,1024]{1,0:T(8,128)(2,1)} %bitcast.7, f32[1152,384]{1,0:T(8,128)} %fusion.23, f32[1152,384]{1,0:T(8,128)} %fusion.24), kind=kOutput, calls=%fused_computation.11 | convolution fusion | flops 909017088 | bytes 6684672 | tf_op jit(solution)/shard_map/dot_general | solution.py:20
  138.2 0.0 copy-done.12
  138.2 0.0 copy-done.13
  138.3 3.8 %multiply_convert_fusion.2 = (bf16[1152,384]{1,0:T(8,128)(2,1)S(1)}, bf16[1152,384]{1,0:T(8,128)(2,1)S(1)}) fusion(f32[1152,384]{1,0:T(8,128)S(1)} %copy-done.13, f32[1152,384]{1,0:T(8,128)S(1)} %copy-done.12, bf16[1152,1024]{1,0:T(8,128)(2,1)} %bitcast.7, bf16[384,1024]{1,0:T(8,128)(2,1)S(1)} %reshape_squeeze.10), kind=kOutput, calls=%fused_computation.7 | convolution fusion | flops 911720448 | bytes 8454144 | tf_op jit(solution)/shard_map/dot_general | solution.py:14
  142.1 0.0 copy-start.4
  142.1 0.0 copy-done.3
  142.1 2.4 convolution_convert_fusion.3
  144.5 0.0 copy-done.4
  144.5 2.4 convolution_convert_fusion.2
  146.9 2.0 stack.15
  149.0 3.1 %copy_bitcast_fusion = bf16[2,8,2,3,32,384]{5,4,3,2,1,0:T(8,128)(2,1)} fusion(bf16[2,8,2,1,32,384]{5,4,2,1,0,3:T(8,128)(2,1)S(1)} %stack.15, bf16[2,8,2,1,32,384]{5,4,2,1,0,3:T(8,128)(2,1)} %bitcast.69, bf16[2,8,2,1,32,384]{5,4,2,1,0,3:T(8,128)(2,1)} %bitcast.68), kind=kLoop, calls=%fused_computation.4 | loop fusion | flops 2359296 | bytes 4718592 | tf_op jit(solution)/shard_map/transpose | solution.py:90
  152.1 0.0 reduce-scatter.4.cloned.1.call-update
  152.1 0.0 copy-start.5
  152.1 1.4 fusion.25
  153.6 0.0 copy-done.5
  153.6 2.9 %fusion = bf16[1152,1024]{1,0:T(8,128)(2,1)} fusion(f32[1152,1024]{1,0:T(8,128)S(1)} %fusion.25, bf16[1152,384]{1,0:T(8,128)(2,1)S(1)} %copy-done.5, bf16[1024,384]{1,0:T(8,128)(2,1)S(1)} %bitcast.60), kind=kOutput, calls=%fused_computation.2 | convolution fusion | flops 908328960 | bytes 8749056 | tf_op jit(solution)/shard_map/dot_general | solution.py:14
  156.5 5.7 %all-to-all-start.2 = ((bf16[16,72,1024]{2,1,0:T(8,128)(2,1)}), bf16[16,72,1024]{2,1,0:T(8,128)(2,1)S(1)}, u32[]{:S(2)}, u32[]{:S(2)}) async-start(bf16[16,72,1024]{2,1,0:T(8,128)(2,1)} %bitcast.58), calls=%async_computation.2 | async-start | bytes 4718592 | tf_op jit(solution)/shard_map/all_to_all | solution.py:76
  162.2 0.0 reduce-scatter.6.cloned.1.call-start
  162.2 12.2 %reduce-scatter.4.cloned.1.call-done = bf16[1,8,2,3,32,384]{5,4,3,2,1,0:T(8,128)(2,1)} async-done(((bf16[2,8,2,3,32,384]{5,4,3,2,1,0:T(8,128)(2,1)}), bf16[1,8,2,3,32,384]{5,4,3,2,1,0:T(8,128)(2,1)}) %reduce-scatter.4.cloned.1.call-update) | async-done | bytes 1179664 | tf_op jit(solution)/shard_map/reduce_scatter | solution.py:91
  174.4 0.0 reduce-scatter.6.cloned.1.call-update
  174.5 0.0 reduce-scatter.8.cloned.1.call-start
  174.5 41.9 %reduce-scatter.6.cloned.1.call-done = bf16[1,1,2,3,32,384]{5,4,3,2,1,0:T(8,128)(2,1)} async-done(((bf16[1,8,2,3,32,384]{5,4,3,2,1,0:T(8,128)(2,1)}), bf16[1,1,2,3,32,384]{5,4,3,2,1,0:T(8,128)(2,1)}) %reduce-scatter.6.cloned.1.call-update) | async-done | bytes 147472 | tf_op jit(solution)/shard_map/reduce_scatter | solution.py:92
  216.4 0.0 reduce-scatter.8.cloned.1.call-update
  216.5 0.4 all-to-all-done.2
  216.9 1.3 fusion.2
  218.1 22.8 %reduce-scatter.8.cloned.1.call-done = bf16[1,1,1,3,32,384]{5,4,3,2,1,0:T(8,128)(2,1)} async-done(((bf16[1,1,2,3,32,384]{5,4,3,2,1,0:T(8,128)(2,1)}), bf16[1,1,1,3,32,384]{5,4,3,2,1,0:T(8,128)(2,1)}) %reduce-scatter.8.cloned.1.call-update) | async-done | bytes 73744 | tf_op jit(solution)/shard_map/reduce_scatter | solution.py:93
  240.9 1.4 convert_multiply_fusion
  242.3 0.7 mul.86
  (13 shorter events, 0.1 us)
Async XLA Ops:
  7.2 1.1 copy-start
  10.5 8.9 %copy-start.7 = (bf16[1,12,1024]{2,1,0:T(8,128)(2,1)S(1)}, bf16[1,12,1024]{2,1,0:T(8,128)(2,1)}, u32[]{:S(2)}) copy-start(bf16[1,12,1024]{2,1,0:T(8,128)(2,1)} %param.13) | copy-start | bytes 73732
  10.5 9.0 %copy-start.8 = (bf16[1,32,384]{2,1,0:T(8,128)(2,1)S(1)}, bf16[1,32,384]{2,1,0:T(8,128)(2,1)}, u32[]{:S(2)}) copy-start(bf16[1,32,384]{2,1,0:T(8,128)(2,1)} %param.12) | copy-start | bytes 73732
  10.5 9.0 %copy-start.9 = (bf16[1,32,384]{2,1,0:T(8,128)(2,1)S(1)}, bf16[1,32,384]{2,1,0:T(8,128)(2,1)}, u32[]{:S(2)}) copy-start(bf16[1,32,384]{2,1,0:T(8,128)(2,1)} %param.11) | copy-start | bytes 73732
  10.5 16.3 %copy-start.10 = (s32[128,8]{0,1:T(8,128)S(1)}, s32[128,8]{0,1:T(8,128)}, u32[]{:S(2)}) copy-start(s32[128,8]{0,1:T(8,128)} %param.9) | copy-start | bytes 12292
  10.5 16.3 %copy-start.11 = (f32[128,8]{0,1:T(8,128)S(1)}, f32[128,8]{0,1:T(8,128)}, u32[]{:S(2)}) copy-start(f32[128,8]{0,1:T(8,128)} %param.10) | copy-start | bytes 12292
  10.5 16.9 %copy-start.6 = (bf16[128,1024]{1,0:T(8,128)(2,1)S(1)}, bf16[128,1024]{1,0:T(8,128)(2,1)}, u32[]{:S(2)}) copy-start(bf16[128,1024]{1,0:T(8,128)(2,1)} %param.8) | copy-start | bytes 786436
  10.5 62.8 %all-to-all-start.1 = ((bf16[16,72,1024]{2,1,0:T(8,128)(2,1)}), bf16[16,72,1024]{2,1,0:T(8,128)(2,1)S(1)}, u32[]{:S(2)}, u32[]{:S(2)}) async-start(bf16[16,72,1024]{2,1,0:T(8,128)(2,1)} %convolution_convert_fusion), calls=%async_computation.1 | async-start | bytes 4718592 | tf_op jit(solution)/shard_map/all_to_all | solution.py:56
  19.4 59.9 %all-gather.4.cloned.1.call-start = ((), (), s32[]{:S(2)}) async-start(), calls=%async_computation.6 | async-start | bytes 1327104 | tf_op jit(solution)/shard_map/all_gather | solution.py:37
  73.3 5.9 %copy-start.1 = (bf16[16,72,1024]{2,1,0:T(8,128)(2,1)}, bf16[16,72,1024]{2,1,0:T(8,128)(2,1)S(1)}, u32[]{:S(2)}) copy-start(bf16[16,72,1024]{2,1,0:T(8,128)(2,1)S(1)} %all-to-all-done.1) | copy-start | bytes 7077892
  73.3 59.9 %all-to-all-start = ((bf16[16,72,1024]{2,1,0:T(8,128)(2,1)}), bf16[16,72,1024]{2,1,0:T(8,128)(2,1)}, u32[]{:S(2)}, u32[]{:S(2)}) async-start(bf16[16,72,1024]{2,1,0:T(8,128)(2,1)} %multiply_convert_fusion), calls=%async_computation | async-start | bytes 4718592 | tf_op jit(solution)/shard_map/all_to_all | solution.py:60
  79.1 28.6 %all-gather.6.cloned.1.call-start = ((), (), s32[]{:S(2)}) async-start(), calls=%async_computation.7 | async-start | bytes 3538944 | tf_op jit(solution)/shard_map/all_gather | solution.py:38
  79.9 94.5 %reduce-scatter.4.cloned.1.call-start = ((), (), s32[]{:S(2)}) async-start(), calls=%async_computation.8 | async-start | bytes 3538944 | tf_op jit(solution)/shard_map/reduce_scatter | solution.py:91
  110.5 4.4 %copy-start.2 = (bf16[16,72,1024]{2,1,0:T(8,128)(2,1)S(1)}, bf16[16,72,1024]{2,1,0:T(8,128)(2,1)}, u32[]{:S(2)}) copy-start(bf16[16,72,1024]{2,1,0:T(8,128)(2,1)} %copy-done.1) | copy-start | bytes 7077892
  133.2 5.0 %copy-start.12 = (f32[1152,384]{1,0:T(8,128)S(1)}, f32[1152,384]{1,0:T(8,128)}, u32[]{:S(2)}) copy-start(f32[1152,384]{1,0:T(8,128)} %fusion.23) | copy-start | bytes 5308420
  133.2 5.0 %copy-start.13 = (f32[1152,384]{1,0:T(8,128)S(1)}, f32[1152,384]{1,0:T(8,128)}, u32[]{:S(2)}) copy-start(f32[1152,384]{1,0:T(8,128)} %fusion.24) | copy-start | bytes 5308420
  138.2 3.9 %copy-start.3 = (bf16[16,72,1024]{2,1,0:T(8,128)(2,1)S(1)}, bf16[16,72,1024]{2,1,0:T(8,128)(2,1)}, u32[]{:S(2)}) copy-start(bf16[16,72,1024]{2,1,0:T(8,128)(2,1)} %copy-done.1) | copy-start | bytes 7077892
  142.1 2.4 copy-start.4
  152.1 1.4 copy-start.5
  156.5 60.4 %all-to-all-start.2 = ((bf16[16,72,1024]{2,1,0:T(8,128)(2,1)}), bf16[16,72,1024]{2,1,0:T(8,128)(2,1)S(1)}, u32[]{:S(2)}, u32[]{:S(2)}) async-start(bf16[16,72,1024]{2,1,0:T(8,128)(2,1)} %bitcast.58), calls=%async_computation.2 | async-start | bytes 4718592 | tf_op jit(solution)/shard_map/all_to_all | solution.py:76
  162.2 54.2 %reduce-scatter.6.cloned.1.call-start = ((), (), s32[]{:S(2)}) async-start(), calls=%async_computation.9 | async-start | bytes 1327104 | tf_op jit(solution)/shard_map/reduce_scatter | solution.py:92
  174.5 66.5 %reduce-scatter.8.cloned.1.call-start = ((), (), s32[]{:S(2)}) async-start(), calls=%async_computation.10 | async-start | bytes 221184 | tf_op jit(solution)/shard_map/reduce_scatter | solution.py:93
Sparse Core Ops, SparseCore 0:
  26.9 41.6 all-gather.3
  82.1 25.6 all-gather.5
  152.3 22.1 reduce-scatter.3
  177.1 39.2 reduce-scatter.5
  219.0 21.8 reduce-scatter.7
